TPU v7x, 256 devices: a whole 4x4x8 slice. The times are simulated.
256 devices in a mesh: ctx: 32 (over z, x), tp: 8 (over y, core).
Axes of the slice: x: 4, y: 4, z: 8, core: 2. Of those that a mesh axis runs over, the one named last changes fastest.
Arguments:
- tokens: bfloat16 [16384, 3072], P(('ctx', 'tp')), may hold values from -6 to 6
- w_query: bfloat16 [3072, 4096], P(None, 'tp'), may hold values from -0.109375 to 0.109375
- w_key: bfloat16 [3072, 4096], P(None, 'tp'), may hold values from -0.109375 to 0.109375
- w_value: bfloat16 [3072, 4096], P(None, 'tp'), may hold values from -0.109375 to 0.109375
- norm_gain: float32 [4096], P('tp'), may hold values from 0.1 to 1.9
Outputs:
- attended: bfloat16 [16384, 4096], P('ctx', 'tp')
All inputs are finite; a program needn't handle non-finite values.
Results may differ from a plain program's by a relative error of at most 0.0062.
Values may be sent and summed in bfloat16 or wider, within the bound.
No kernel may reach another device: no remote copies, remote signals or barrier semaphores. Data moves between devices by JAX's collectives and lax.ppermute only.
A program may use at most 64 MiB of HBM per device.

v0:
```python
import jax
import jax.numpy as jnp
from jax import lax
from jax.sharding import PartitionSpec as P

HEAD_DIM = 128
BLOCK = 512
EPSILON = 1e-06


def from_behind(value, axis, by):
    size = lax.axis_size(axis)
    pairs = [(i, i + by) for i in range(size) if 0 <= i + by < size]
    return lax.ppermute(value, axis, pairs)


def body(tokens, w_query, w_key, w_value, norm_gain):
    local_width = w_query.shape[1]
    head_count = local_width // HEAD_DIM
    piece_rows = lax.all_gather(tokens, "tp", axis=0, tiled=True)
    query_part = jnp.dot(piece_rows, w_query, preferred_element_type=jnp.float32).astype(
        jnp.bfloat16
    )
    key_part = jnp.dot(piece_rows, w_key, preferred_element_type=jnp.float32).astype(jnp.bfloat16)
    value_part = jnp.dot(piece_rows, w_value, preferred_element_type=jnp.float32).astype(
        jnp.bfloat16
    )
    projected = jnp.concatenate([query_part, key_part, value_part], axis=1)
    group_len = projected.shape[0]
    block_count = group_len // BLOCK
    shaped = projected.reshape(block_count, BLOCK, 3, head_count, HEAD_DIM)
    query_rows = shaped[:, :, 0]
    key_rows = shaped[:, :, 1]
    value_rows = shaped[:, :, 2]
    block_states = jnp.einsum(
        "bshd,bshe->bhde", key_rows, value_rows, preferred_element_type=jnp.float32
    )
    local_state = jnp.sum(block_states, axis=0)
    empty_state = jnp.zeros_like(local_state)

    def advance(step_index, carried):
        return from_behind(carried + local_state, "ctx", 1)

    prefix_state = lax.fori_loop(0, lax.axis_size("ctx") - 1, advance, empty_state)
    running = jnp.cumsum(block_states, axis=0)
    earlier = jnp.concatenate([jnp.zeros_like(block_states), running[:-1]], axis=0)
    block_start = prefix_state[None] + earlier
    scores = jnp.einsum("bqhd,bkhd->bhqk", query_rows, key_rows, preferred_element_type=jnp.float32)
    causal = jnp.arange(BLOCK)[:, None] >= jnp.arange(BLOCK)[None, :]
    scores = jnp.where(causal[None, None], scores, jnp.float32(0.0)).astype(jnp.bfloat16)
    inner = jnp.einsum("bhqk,bkhe->bqhe", scores, value_rows, preferred_element_type=jnp.float32)
    carried_part = jnp.einsum(
        "bqhd,bhde->bqhe",
        query_rows.astype(jnp.float32),
        block_start,
        precision=lax.Precision.HIGHEST,
    )
    mixed = inner + carried_part
    mean_square = jnp.mean(mixed * mixed, axis=-1, keepdims=True)
    normed = mixed * lax.rsqrt(mean_square + EPSILON) * norm_gain.reshape(head_count, HEAD_DIM)
    return normed.reshape(group_len, local_width).astype(jnp.bfloat16)


def solution(mesh):
    placed = (P(("ctx", "tp"), None), P(None, "tp"), P(None, "tp"), P(None, "tp"), P("tp"))
    return jax.shard_map(
        body, mesh=mesh, in_specs=placed, out_specs=P("ctx", "tp"), check_vma=False
    )
```

profile of v0, /device:TPU:128, one launch (start us, length us, event | category | flops | bytes accessed | tf_op | source)
XLA Modules:
  0.0 505.0 jit_solution(23542777974359117)
XLA Ops:
  8.0 32.9 %all-gather.2.cloned.1.call-done = bf16[512,3072]{1,0:T(8,128)(2,1)} async-done(((bf16[64,3072]{1,0:T(8,128)(2,1)}), bf16[512,3072]{1,0:T(8,128)(2,1)}) %all-gather.2.cloned.1.call-update) | async-done | bytes 3145744 | tf_op jit(solution)/shard_map/all_gather | solution.py:20
  50.9 436.2 %while.10 = (s32[]{:T(128)}, f32[4,128,128]{2,1,0:T(8,128)S(1)}, f32[4,128,128]{2,1,0:T(8,128)}, s32[]{:T(128)}) while((s32[]{:T(128)}, f32[4,128,128]{2,1,0:T(8,128)S(1)}, f32[4,128,128]{2,1,0:T(8,128)}, s32[]{:T(128)}) %tuple.19), condition=%wide.region_1.0_spmd, body=%wide.region_0.0_spmd.sunk | while | flops 65538 | bytes 1835101 | solution.py:44
  56.0 10.5 %collective-permute-done = f32[4,128,128]{2,1,0:T(8,128)S(1)} collective-permute-done((f32[4,128,128]{2,1,0:T(8,128)}, f32[4,128,128]{2,1,0:T(8,128)S(1)}, u32[]{:S(2)}, u32[]{:S(2)}) %collective-permute-start) | collective-permute-done | bytes 262176 | tf_op jit(solution)/shard_map/while/body/eval_jaxpr/ppermute | solution.py:14
  70.0 11.1 %collective-permute-done = f32[4,128,128]{2,1,0:T(8,128)S(1)} collective-permute-done((f32[4,128,128]{2,1,0:T(8,128)}, f32[4,128,128]{2,1,0:T(8,128)S(1)}, u32[]{:S(2)}, u32[]{:S(2)}) %collective-permute-start) | collective-permute-done | bytes 262176 | tf_op jit(solution)/shard_map/while/body/eval_jaxpr/ppermute | solution.py:14
  84.7 10.2 %collective-permute-done = f32[4,128,128]{2,1,0:T(8,128)S(1)} collective-permute-done((f32[4,128,128]{2,1,0:T(8,128)}, f32[4,128,128]{2,1,0:T(8,128)S(1)}, u32[]{:S(2)}, u32[]{:S(2)}) %collective-permute-start) | collective-permute-done | bytes 262176 | tf_op jit(solution)/shard_map/while/body/eval_jaxpr/ppermute | solution.py:14
  98.5 9.9 %collective-permute-done = f32[4,128,128]{2,1,0:T(8,128)S(1)} collective-permute-done((f32[4,128,128]{2,1,0:T(8,128)}, f32[4,128,128]{2,1,0:T(8,128)S(1)}, u32[]{:S(2)}, u32[]{:S(2)}) %collective-permute-start) | collective-permute-done | bytes 262176 | tf_op jit(solution)/shard_map/while/body/eval_jaxpr/ppermute | solution.py:14
  112.0 9.9 %collective-permute-done = f32[4,128,128]{2,1,0:T(8,128)S(1)} collective-permute-done((f32[4,128,128]{2,1,0:T(8,128)}, f32[4,128,128]{2,1,0:T(8,128)S(1)}, u32[]{:S(2)}, u32[]{:S(2)}) %collective-permute-start) | collective-permute-done | bytes 262176 | tf_op jit(solution)/shard_map/while/body/eval_jaxpr/ppermute | solution.py:14
  165.8 9.9 %collective-permute-done = f32[4,128,128]{2,1,0:T(8,128)S(1)} collective-permute-done((f32[4,128,128]{2,1,0:T(8,128)}, f32[4,128,128]{2,1,0:T(8,128)S(1)}, u32[]{:S(2)}, u32[]{:S(2)}) %collective-permute-start) | collective-permute-done | bytes 262176 | tf_op jit(solution)/shard_map/while/body/eval_jaxpr/ppermute | solution.py:14
  179.3 10.6 %collective-permute-done = f32[4,128,128]{2,1,0:T(8,128)S(1)} collective-permute-done((f32[4,128,128]{2,1,0:T(8,128)}, f32[4,128,128]{2,1,0:T(8,128)S(1)}, u32[]{:S(2)}, u32[]{:S(2)}) %collective-permute-start) | collective-permute-done | bytes 262176 | tf_op jit(solution)/shard_map/while/body/eval_jaxpr/ppermute | solution.py:14
  193.4 11.7 %collective-permute-done = f32[4,128,128]{2,1,0:T(8,128)S(1)} collective-permute-done((f32[4,128,128]{2,1,0:T(8,128)}, f32[4,128,128]{2,1,0:T(8,128)S(1)}, u32[]{:S(2)}, u32[]{:S(2)}) %collective-permute-start) | collective-permute-done | bytes 262176 | tf_op jit(solution)/shard_map/while/body/eval_jaxpr/ppermute | solution.py:14
  208.7 12.5 %collective-permute-done = f32[4,128,128]{2,1,0:T(8,128)S(1)} collective-permute-done((f32[4,128,128]{2,1,0:T(8,128)}, f32[4,128,128]{2,1,0:T(8,128)S(1)}, u32[]{:S(2)}, u32[]{:S(2)}) %collective-permute-start) | collective-permute-done | bytes 262176 | tf_op jit(solution)/shard_map/while/body/eval_jaxpr/ppermute | solution.py:14
  224.8 11.6 %collective-permute-done = f32[4,128,128]{2,1,0:T(8,128)S(1)} collective-permute-done((f32[4,128,128]{2,1,0:T(8,128)}, f32[4,128,128]{2,1,0:T(8,128)S(1)}, u32[]{:S(2)}, u32[]{:S(2)}) %collective-permute-start) | collective-permute-done | bytes 262176 | tf_op jit(solution)/shard_map/while/body/eval_jaxpr/ppermute | solution.py:14
  240.0 10.8 %collective-permute-done = f32[4,128,128]{2,1,0:T(8,128)S(1)} collective-permute-done((f32[4,128,128]{2,1,0:T(8,128)}, f32[4,128,128]{2,1,0:T(8,128)S(1)}, u32[]{:S(2)}, u32[]{:S(2)}) %collective-permute-start) | collective-permute-done | bytes 262176 | tf_op jit(solution)/shard_map/while/body/eval_jaxpr/ppermute | solution.py:14
  254.4 9.9 %collective-permute-done = f32[4,128,128]{2,1,0:T(8,128)S(1)} collective-permute-done((f32[4,128,128]{2,1,0:T(8,128)}, f32[4,128,128]{2,1,0:T(8,128)S(1)}, u32[]{:S(2)}, u32[]{:S(2)}) %collective-permute-start) | collective-permute-done | bytes 262176 | tf_op jit(solution)/shard_map/while/body/eval_jaxpr/ppermute | solution.py:14
  267.9 9.9 %collective-permute-done = f32[4,128,128]{2,1,0:T(8,128)S(1)} collective-permute-done((f32[4,128,128]{2,1,0:T(8,128)}, f32[4,128,128]{2,1,0:T(8,128)S(1)}, u32[]{:S(2)}, u32[]{:S(2)}) %collective-permute-start) | collective-permute-done | bytes 262176 | tf_op jit(solution)/shard_map/while/body/eval_jaxpr/ppermute | solution.py:14
  281.3 9.9 %collective-permute-done = f32[4,128,128]{2,1,0:T(8,128)S(1)} collective-permute-done((f32[4,128,128]{2,1,0:T(8,128)}, f32[4,128,128]{2,1,0:T(8,128)S(1)}, u32[]{:S(2)}, u32[]{:S(2)}) %collective-permute-start) | collective-permute-done | bytes 262176 | tf_op jit(solution)/shard_map/while/body/eval_jaxpr/ppermute | solution.py:14
  294.8 9.9 %collective-permute-done = f32[4,128,128]{2,1,0:T(8,128)S(1)} collective-permute-done((f32[4,128,128]{2,1,0:T(8,128)}, f32[4,128,128]{2,1,0:T(8,128)S(1)}, u32[]{:S(2)}, u32[]{:S(2)}) %collective-permute-start) | collective-permute-done | bytes 262176 | tf_op jit(solution)/shard_map/while/body/eval_jaxpr/ppermute | solution.py:14
  348.6 10.9 %collective-permute-done = f32[4,128,128]{2,1,0:T(8,128)S(1)} collective-permute-done((f32[4,128,128]{2,1,0:T(8,128)}, f32[4,128,128]{2,1,0:T(8,128)S(1)}, u32[]{:S(2)}, u32[]{:S(2)}) %collective-permute-start) | collective-permute-done | bytes 262176 | tf_op jit(solution)/shard_map/while/body/eval_jaxpr/ppermute | solution.py:14
  363.1 12.0 %collective-permute-done = f32[4,128,128]{2,1,0:T(8,128)S(1)} collective-permute-done((f32[4,128,128]{2,1,0:T(8,128)}, f32[4,128,128]{2,1,0:T(8,128)S(1)}, u32[]{:S(2)}, u32[]{:S(2)}) %collective-permute-start) | collective-permute-done | bytes 262176 | tf_op jit(solution)/shard_map/while/body/eval_jaxpr/ppermute | solution.py:14
  378.7 12.2 %collective-permute-done = f32[4,128,128]{2,1,0:T(8,128)S(1)} collective-permute-done((f32[4,128,128]{2,1,0:T(8,128)}, f32[4,128,128]{2,1,0:T(8,128)S(1)}, u32[]{:S(2)}, u32[]{:S(2)}) %collective-permute-start) | collective-permute-done | bytes 262176 | tf_op jit(solution)/shard_map/while/body/eval_jaxpr/ppermute | solution.py:14
  394.5 11.3 %collective-permute-done = f32[4,128,128]{2,1,0:T(8,128)S(1)} collective-permute-done((f32[4,128,128]{2,1,0:T(8,128)}, f32[4,128,128]{2,1,0:T(8,128)S(1)}, u32[]{:S(2)}, u32[]{:S(2)}) %collective-permute-start) | collective-permute-done | bytes 262176 | tf_op jit(solution)/shard_map/while/body/eval_jaxpr/ppermute | solution.py:14
  409.4 10.5 %collective-permute-done = f32[4,128,128]{2,1,0:T(8,128)S(1)} collective-permute-done((f32[4,128,128]{2,1,0:T(8,128)}, f32[4,128,128]{2,1,0:T(8,128)S(1)}, u32[]{:S(2)}, u32[]{:S(2)}) %collective-permute-start) | collective-permute-done | bytes 262176 | tf_op jit(solution)/shard_map/while/body/eval_jaxpr/ppermute | solution.py:14
  463.8 9.9 %collective-permute-done = f32[4,128,128]{2,1,0:T(8,128)S(1)} collective-permute-done((f32[4,128,128]{2,1,0:T(8,128)}, f32[4,128,128]{2,1,0:T(8,128)S(1)}, u32[]{:S(2)}, u32[]{:S(2)}) %collective-permute-start) | collective-permute-done | bytes 262176 | tf_op jit(solution)/shard_map/while/body/eval_jaxpr/ppermute | solution.py:14
  477.3 9.9 %collective-permute-done = f32[4,128,128]{2,1,0:T(8,128)S(1)} collective-permute-done((f32[4,128,128]{2,1,0:T(8,128)}, f32[4,128,128]{2,1,0:T(8,128)S(1)}, u32[]{:S(2)}, u32[]{:S(2)}) %collective-permute-start) | collective-permute-done | bytes 262176 | tf_op jit(solution)/shard_map/while/body/eval_jaxpr/ppermute | solution.py:14
  (97 shorter events, 223.5 us)
Async XLA Ops:
  6.5 34.4 %all-gather.2.cloned.1.call-start = ((), (), s32[]{:S(2)}) async-start(), calls=%async_computation | async-start | bytes 3538944 | tf_op jit(solution)/shard_map/all_gather | solution.py:20
  52.6 13.9 %collective-permute-start = (f32[4,128,128]{2,1,0:T(8,128)}, f32[4,128,128]{2,1,0:T(8,128)S(1)}, u32[]{:S(2)}, u32[]{:S(2)}) collective-permute-start(f32[4,128,128]{2,1,0:T(8,128)} %add.39), channel_id=1, source_target_pairs={{0,8},{8,16},{16,24},{24,32},{32,40},{40,48},{48,56},{56,64},{64,7... | collective-permute-start | bytes 786440 | tf_op jit(solution)/shard_map/while/body/eval_jaxpr/ppermute | solution.py:14
  68.1 13.0 %collective-permute-start = (f32[4,128,128]{2,1,0:T(8,128)}, f32[4,128,128]{2,1,0:T(8,128)S(1)}, u32[]{:S(2)}, u32[]{:S(2)}) collective-permute-start(f32[4,128,128]{2,1,0:T(8,128)} %add.39), channel_id=1, source_target_pairs={{0,8},{8,16},{16,24},{24,32},{32,40},{40,48},{48,56},{56,64},{64,7... | collective-permute-start | bytes 786440 | tf_op jit(solution)/shard_map/while/body/eval_jaxpr/ppermute | solution.py:14
  82.8 12.1 %collective-permute-start = (f32[4,128,128]{2,1,0:T(8,128)}, f32[4,128,128]{2,1,0:T(8,128)S(1)}, u32[]{:S(2)}, u32[]{:S(2)}) collective-permute-start(f32[4,128,128]{2,1,0:T(8,128)} %add.39), channel_id=1, source_target_pairs={{0,8},{8,16},{16,24},{24,32},{32,40},{40,48},{48,56},{56,64},{64,7... | collective-permute-start | bytes 786440 | tf_op jit(solution)/shard_map/while/body/eval_jaxpr/ppermute | solution.py:14
  96.6 11.8 %collective-permute-start = (f32[4,128,128]{2,1,0:T(8,128)}, f32[4,128,128]{2,1,0:T(8,128)S(1)}, u32[]{:S(2)}, u32[]{:S(2)}) collective-permute-start(f32[4,128,128]{2,1,0:T(8,128)} %add.39), channel_id=1, source_target_pairs={{0,8},{8,16},{16,24},{24,32},{32,40},{40,48},{48,56},{56,64},{64,7... | collective-permute-start | bytes 786440 | tf_op jit(solution)/shard_map/while/body/eval_jaxpr/ppermute | solution.py:14
  110.1 11.8 %collective-permute-start = (f32[4,128,128]{2,1,0:T(8,128)}, f32[4,128,128]{2,1,0:T(8,128)S(1)}, u32[]{:S(2)}, u32[]{:S(2)}) collective-permute-start(f32[4,128,128]{2,1,0:T(8,128)} %add.39), channel_id=1, source_target_pairs={{0,8},{8,16},{16,24},{24,32},{32,40},{40,48},{48,56},{56,64},{64,7... | collective-permute-start | bytes 786440 | tf_op jit(solution)/shard_map/while/body/eval_jaxpr/ppermute | solution.py:14
  123.5 11.8 %collective-permute-start = (f32[4,128,128]{2,1,0:T(8,128)}, f32[4,128,128]{2,1,0:T(8,128)S(1)}, u32[]{:S(2)}, u32[]{:S(2)}) collective-permute-start(f32[4,128,128]{2,1,0:T(8,128)} %add.39), channel_id=1, source_target_pairs={{0,8},{8,16},{16,24},{24,32},{32,40},{40,48},{48,56},{56,64},{64,7... | collective-permute-start | bytes 786440 | tf_op jit(solution)/shard_map/while/body/eval_jaxpr/ppermute | solution.py:14
  137.0 11.8 %collective-permute-start = (f32[4,128,128]{2,1,0:T(8,128)}, f32[4,128,128]{2,1,0:T(8,128)S(1)}, u32[]{:S(2)}, u32[]{:S(2)}) collective-permute-start(f32[4,128,128]{2,1,0:T(8,128)} %add.39), channel_id=1, source_target_pairs={{0,8},{8,16},{16,24},{24,32},{32,40},{40,48},{48,56},{56,64},{64,7... | collective-permute-start | bytes 786440 | tf_op jit(solution)/shard_map/while/body/eval_jaxpr/ppermute | solution.py:14
  150.4 11.8 %collective-permute-start = (f32[4,128,128]{2,1,0:T(8,128)}, f32[4,128,128]{2,1,0:T(8,128)S(1)}, u32[]{:S(2)}, u32[]{:S(2)}) collective-permute-start(f32[4,128,128]{2,1,0:T(8,128)} %add.39), channel_id=1, source_target_pairs={{0,8},{8,16},{16,24},{24,32},{32,40},{40,48},{48,56},{56,64},{64,7... | collective-permute-start | bytes 786440 | tf_op jit(solution)/shard_map/while/body/eval_jaxpr/ppermute | solution.py:14
  163.9 11.8 %collective-permute-start = (f32[4,128,128]{2,1,0:T(8,128)}, f32[4,128,128]{2,1,0:T(8,128)S(1)}, u32[]{:S(2)}, u32[]{:S(2)}) collective-permute-start(f32[4,128,128]{2,1,0:T(8,128)} %add.39), channel_id=1, source_target_pairs={{0,8},{8,16},{16,24},{24,32},{32,40},{40,48},{48,56},{56,64},{64,7... | collective-permute-start | bytes 786440 | tf_op jit(solution)/shard_map/while/body/eval_jaxpr/ppermute | solution.py:14
  177.3 12.5 %collective-permute-start = (f32[4,128,128]{2,1,0:T(8,128)}, f32[4,128,128]{2,1,0:T(8,128)S(1)}, u32[]{:S(2)}, u32[]{:S(2)}) collective-permute-start(f32[4,128,128]{2,1,0:T(8,128)} %add.39), channel_id=1, source_target_pairs={{0,8},{8,16},{16,24},{24,32},{32,40},{40,48},{48,56},{56,64},{64,7... | collective-permute-start | bytes 786440 | tf_op jit(solution)/shard_map/while/body/eval_jaxpr/ppermute | solution.py:14
  191.5 13.6 %collective-permute-start = (f32[4,128,128]{2,1,0:T(8,128)}, f32[4,128,128]{2,1,0:T(8,128)S(1)}, u32[]{:S(2)}, u32[]{:S(2)}) collective-permute-start(f32[4,128,128]{2,1,0:T(8,128)} %add.39), channel_id=1, source_target_pairs={{0,8},{8,16},{16,24},{24,32},{32,40},{40,48},{48,56},{56,64},{64,7... | collective-permute-start | bytes 786440 | tf_op jit(solution)/shard_map/while/body/eval_jaxpr/ppermute | solution.py:14
  206.8 14.4 %collective-permute-start = (f32[4,128,128]{2,1,0:T(8,128)}, f32[4,128,128]{2,1,0:T(8,128)S(1)}, u32[]{:S(2)}, u32[]{:S(2)}) collective-permute-start(f32[4,128,128]{2,1,0:T(8,128)} %add.39), channel_id=1, source_target_pairs={{0,8},{8,16},{16,24},{24,32},{32,40},{40,48},{48,56},{56,64},{64,7... | collective-permute-start | bytes 786440 | tf_op jit(solution)/shard_map/while/body/eval_jaxpr/ppermute | solution.py:14
  222.9 13.6 %collective-permute-start = (f32[4,128,128]{2,1,0:T(8,128)}, f32[4,128,128]{2,1,0:T(8,128)S(1)}, u32[]{:S(2)}, u32[]{:S(2)}) collective-permute-start(f32[4,128,128]{2,1,0:T(8,128)} %add.39), channel_id=1, source_target_pairs={{0,8},{8,16},{16,24},{24,32},{32,40},{40,48},{48,56},{56,64},{64,7... | collective-permute-start | bytes 786440 | tf_op jit(solution)/shard_map/while/body/eval_jaxpr/ppermute | solution.py:14
  238.1 12.7 %collective-permute-start = (f32[4,128,128]{2,1,0:T(8,128)}, f32[4,128,128]{2,1,0:T(8,128)S(1)}, u32[]{:S(2)}, u32[]{:S(2)}) collective-permute-start(f32[4,128,128]{2,1,0:T(8,128)} %add.39), channel_id=1, source_target_pairs={{0,8},{8,16},{16,24},{24,32},{32,40},{40,48},{48,56},{56,64},{64,7... | collective-permute-start | bytes 786440 | tf_op jit(solution)/shard_map/while/body/eval_jaxpr/ppermute | solution.py:14
  252.5 11.8 %collective-permute-start = (f32[4,128,128]{2,1,0:T(8,128)}, f32[4,128,128]{2,1,0:T(8,128)S(1)}, u32[]{:S(2)}, u32[]{:S(2)}) collective-permute-start(f32[4,128,128]{2,1,0:T(8,128)} %add.39), channel_id=1, source_target_pairs={{0,8},{8,16},{16,24},{24,32},{32,40},{40,48},{48,56},{56,64},{64,7... | collective-permute-start | bytes 786440 | tf_op jit(solution)/shard_map/while/body/eval_jaxpr/ppermute | solution.py:14
  266.0 11.8 %collective-permute-start = (f32[4,128,128]{2,1,0:T(8,128)}, f32[4,128,128]{2,1,0:T(8,128)S(1)}, u32[]{:S(2)}, u32[]{:S(2)}) collective-permute-start(f32[4,128,128]{2,1,0:T(8,128)} %add.39), channel_id=1, source_target_pairs={{0,8},{8,16},{16,24},{24,32},{32,40},{40,48},{48,56},{56,64},{64,7... | collective-permute-start | bytes 786440 | tf_op jit(solution)/shard_map/while/body/eval_jaxpr/ppermute | solution.py:14
  279.4 11.8 %collective-permute-start = (f32[4,128,128]{2,1,0:T(8,128)}, f32[4,128,128]{2,1,0:T(8,128)S(1)}, u32[]{:S(2)}, u32[]{:S(2)}) collective-permute-start(f32[4,128,128]{2,1,0:T(8,128)} %add.39), channel_id=1, source_target_pairs={{0,8},{8,16},{16,24},{24,32},{32,40},{40,48},{48,56},{56,64},{64,7... | collective-permute-start | bytes 786440 | tf_op jit(solution)/shard_map/while/body/eval_jaxpr/ppermute | solution.py:14
  346.7 12.8 %collective-permute-start = (f32[4,128,128]{2,1,0:T(8,128)}, f32[4,128,128]{2,1,0:T(8,128)S(1)}, u32[]{:S(2)}, u32[]{:S(2)}) collective-permute-start(f32[4,128,128]{2,1,0:T(8,128)} %add.39), channel_id=1, source_target_pairs={{0,8},{8,16},{16,24},{24,32},{32,40},{40,48},{48,56},{56,64},{64,7... | collective-permute-start | bytes 786440 | tf_op jit(solution)/shard_map/while/body/eval_jaxpr/ppermute | solution.py:14
  361.2 13.9 %collective-permute-start = (f32[4,128,128]{2,1,0:T(8,128)}, f32[4,128,128]{2,1,0:T(8,128)S(1)}, u32[]{:S(2)}, u32[]{:S(2)}) collective-permute-start(f32[4,128,128]{2,1,0:T(8,128)} %add.39), channel_id=1, source_target_pairs={{0,8},{8,16},{16,24},{24,32},{32,40},{40,48},{48,56},{56,64},{64,7... | collective-permute-start | bytes 786440 | tf_op jit(solution)/shard_map/while/body/eval_jaxpr/ppermute | solution.py:14
  376.8 14.1 %collective-permute-start = (f32[4,128,128]{2,1,0:T(8,128)}, f32[4,128,128]{2,1,0:T(8,128)S(1)}, u32[]{:S(2)}, u32[]{:S(2)}) collective-permute-start(f32[4,128,128]{2,1,0:T(8,128)} %add.39), channel_id=1, source_target_pairs={{0,8},{8,16},{16,24},{24,32},{32,40},{40,48},{48,56},{56,64},{64,7... | collective-permute-start | bytes 786440 | tf_op jit(solution)/shard_map/while/body/eval_jaxpr/ppermute | solution.py:14
  392.5 13.2 %collective-permute-start = (f32[4,128,128]{2,1,0:T(8,128)}, f32[4,128,128]{2,1,0:T(8,128)S(1)}, u32[]{:S(2)}, u32[]{:S(2)}) collective-permute-start(f32[4,128,128]{2,1,0:T(8,128)} %add.39), channel_id=1, source_target_pairs={{0,8},{8,16},{16,24},{24,32},{32,40},{40,48},{48,56},{56,64},{64,7... | collective-permute-start | bytes 786440 | tf_op jit(solution)/shard_map/while/body/eval_jaxpr/ppermute | solution.py:14
  407.5 12.4 %collective-permute-start = (f32[4,128,128]{2,1,0:T(8,128)}, f32[4,128,128]{2,1,0:T(8,128)S(1)}, u32[]{:S(2)}, u32[]{:S(2)}) collective-permute-start(f32[4,128,128]{2,1,0:T(8,128)} %add.39), channel_id=1, source_target_pairs={{0,8},{8,16},{16,24},{24,32},{32,40},{40,48},{48,56},{56,64},{64,7... | collective-permute-start | bytes 786440 | tf_op jit(solution)/shard_map/while/body/eval_jaxpr/ppermute | solution.py:14
  461.9 11.8 %collective-permute-start = (f32[4,128,128]{2,1,0:T(8,128)}, f32[4,128,128]{2,1,0:T(8,128)S(1)}, u32[]{:S(2)}, u32[]{:S(2)}) collective-permute-start(f32[4,128,128]{2,1,0:T(8,128)} %add.39), channel_id=1, source_target_pairs={{0,8},{8,16},{16,24},{24,32},{32,40},{40,48},{48,56},{56,64},{64,7... | collective-permute-start | bytes 786440 | tf_op jit(solution)/shard_map/while/body/eval_jaxpr/ppermute | solution.py:14
  (14 other events, 143.7 us)
Sparse Core Ops, SparseCore 0:
  9.2 31.7 all-gather.1
where the time goes:
time: 507 us; the launch traced here: 505 us
  waiting for transfers between devices  357 us (70%)
  starting transfers between devices  60.6 us (12%)
  other arithmetic  54.9 us (11%)
  matrix products  15.3 us (3%)
  between operations  13.5 us (3%)
    ppermute x31, waiting for transfers between devices, from_behind(): return lax.ppermute(value, axis, pairs)  323 us
    ppermute x31, starting transfers between devices, from_behind(): return lax.ppermute(value, axis, pairs)  60.6 us
    add x31, other arithmetic, advance(): return from_behind(carried + local_state, 'ctx', 1)  51.8 us
    all_gather x1, waiting for transfers between devices, body(): piece_rows = lax.all_gather(tokens, 'tp', axis=0, tiled=True)  32.9 us
  transfers between devices with their start and end apart: 32, of which 32 were waited for; matrix products, arithmetic and copies ran while one was open for 0% of the time, Pallas kernels for 0%

commit v1 on v0

--- a/solution.py
+++ b/solution.py
@@ -17,7 +17,23 @@
 def body(tokens, w_query, w_key, w_value, norm_gain):
     local_width = w_query.shape[1]
     head_count = local_width // HEAD_DIM
-    piece_rows = lax.all_gather(tokens, "tp", axis=0, tiled=True)
+    count, index, rows = (lax.axis_size("tp"), lax.axis_index("tp"), tokens.shape[0])
+    upward = [(i_2, (i_2 + 1) % count) for i_2 in range(count)]
+    left = [(i_2, (i_2 - 1) % count) for i_2 in range(count)]
+    piece_rows = jnp.zeros((*tokens.shape[:0], count * rows, *tokens.shape[0 + 1 :]), tokens.dtype)
+    piece_rows = lax.dynamic_update_slice_in_dim(piece_rows, tokens, index * rows, axis=0)
+    from_left = from_right = tokens
+    halfway = count // 2
+    for step in range(1, halfway + 1):
+        from_left = lax.ppermute(from_left, "tp", upward)
+        piece_rows = lax.dynamic_update_slice_in_dim(
+            piece_rows, from_left, (index - step) % count * rows, axis=0
+        )
+        if step < count - halfway:
+            from_right = lax.ppermute(from_right, "tp", left)
+            piece_rows = lax.dynamic_update_slice_in_dim(
+                piece_rows, from_right, (index + step) % count * rows, axis=0
+            )
     query_part = jnp.dot(piece_rows, w_query, preferred_element_type=jnp.float32).astype(
         jnp.bfloat16
     )

time: 507 us -> 491 us (0.968)
  between operations: 13.5 us -> 0.16 us
  waiting for transfers between devices: 357 us -> 344 us
  starting transfers between devices: 60.6 us -> 69.5 us
    all_gather x1 -> x0, waiting for transfers between devices: 32.9 us -> none  [body(): piece_rows = lax.all_gather(tokens, 'tp', axis=0, tiled=True)]
    ppermute x0 -> x7, waiting for transfers between devices: none -> 21.9 us  [the longest x4 21.9 us: body(): from_left = lax.ppermute(from_left, 'tp', upward)]
    ppermute x0 -> x7, starting transfers between devices: none -> 8.87 us  [the longest x3 8.86 us: body(): from_right = lax.ppermute(from_right, 'tp', left)]
  transfers between devices with their start and end apart: 32 -> 38, of which waited for: 32 -> 35; matrix products, arithmetic and copies ran while one was open for 0% -> 1% of each run, Pallas kernels for 0% -> 0%
where the time goes in v1:
time: 491 us; the launch traced here: 488 us
  waiting for transfers between devices  344 us (70%)
  starting transfers between devices  69.5 us (14%)
  other arithmetic  55.2 us (11%)
  matrix products  13.3 us (3%)
  local copies, waits for them, and re-layouts  5.9 us (1%)
    ppermute x31, waiting for transfers between devices, from_behind(): return lax.ppermute(value, axis, pairs)  322 us
    ppermute x31, starting transfers between devices, from_behind(): return lax.ppermute(value, axis, pairs)  60.6 us
    add x31, other arithmetic, advance(): return from_behind(carried + local_state, 'ctx', 1)  52.1 us
    ppermute x4, waiting for transfers between devices, body(): from_left = lax.ppermute(from_left, 'tp', upward)  21.9 us
  transfers between devices with their start and end apart: 38, of which 35 were waited for; matrix products, arithmetic and copies ran while one was open for 1% of the time, Pallas kernels for 0%

profile of v1, /device:TPU:128, one launch (start us, length us, event | category | flops | bytes accessed | tf_op | source)
XLA Modules:
  0.0 488.3 jit_solution(6461197437324007264)
XLA Ops:
  42.1 435.1 %while.10 = (s32[]{:T(128)}, f32[4,128,128]{2,1,0:T(8,128)S(1)}, f32[4,128,128]{2,1,0:T(8,128)}, s32[]{:T(128)}) while((s32[]{:T(128)}, f32[4,128,128]{2,1,0:T(8,128)S(1)}, f32[4,128,128]{2,1,0:T(8,128)}, s32[]{:T(128)}) %tuple.19), condition=%wide.region_1.2_spmd, body=%wide.region_0.1_spmd.sunk | while | flops 65538 | bytes 1835101 | solution.py:60
  59.2 9.9 %collective-permute-done = f32[4,128,128]{2,1,0:T(8,128)S(1)} collective-permute-done((f32[4,128,128]{2,1,0:T(8,128)}, f32[4,128,128]{2,1,0:T(8,128)S(1)}, u32[]{:S(2)}, u32[]{:S(2)}) %collective-permute-start) | collective-permute-done | bytes 262176 | tf_op jit(solution)/shard_map/while/body/eval_jaxpr/ppermute | solution.py:14
  72.7 9.9 %collective-permute-done = f32[4,128,128]{2,1,0:T(8,128)S(1)} collective-permute-done((f32[4,128,128]{2,1,0:T(8,128)}, f32[4,128,128]{2,1,0:T(8,128)S(1)}, u32[]{:S(2)}, u32[]{:S(2)}) %collective-permute-start) | collective-permute-done | bytes 262176 | tf_op jit(solution)/shard_map/while/body/eval_jaxpr/ppermute | solution.py:14
  86.2 10.4 %collective-permute-done = f32[4,128,128]{2,1,0:T(8,128)S(1)} collective-permute-done((f32[4,128,128]{2,1,0:T(8,128)}, f32[4,128,128]{2,1,0:T(8,128)S(1)}, u32[]{:S(2)}, u32[]{:S(2)}) %collective-permute-start) | collective-permute-done | bytes 262176 | tf_op jit(solution)/shard_map/while/body/eval_jaxpr/ppermute | solution.py:14
  100.2 11.5 %collective-permute-done = f32[4,128,128]{2,1,0:T(8,128)S(1)} collective-permute-done((f32[4,128,128]{2,1,0:T(8,128)}, f32[4,128,128]{2,1,0:T(8,128)S(1)}, u32[]{:S(2)}, u32[]{:S(2)}) %collective-permute-start) | collective-permute-done | bytes 262176 | tf_op jit(solution)/shard_map/while/body/eval_jaxpr/ppermute | solution.py:14
  115.3 12.6 %collective-permute-done = f32[4,128,128]{2,1,0:T(8,128)S(1)} collective-permute-done((f32[4,128,128]{2,1,0:T(8,128)}, f32[4,128,128]{2,1,0:T(8,128)S(1)}, u32[]{:S(2)}, u32[]{:S(2)}) %collective-permute-start) | collective-permute-done | bytes 262176 | tf_op jit(solution)/shard_map/while/body/eval_jaxpr/ppermute | solution.py:14
  131.6 11.8 %collective-permute-done = f32[4,128,128]{2,1,0:T(8,128)S(1)} collective-permute-done((f32[4,128,128]{2,1,0:T(8,128)}, f32[4,128,128]{2,1,0:T(8,128)S(1)}, u32[]{:S(2)}, u32[]{:S(2)}) %collective-permute-start) | collective-permute-done | bytes 262176 | tf_op jit(solution)/shard_map/while/body/eval_jaxpr/ppermute | solution.py:14
  147.0 10.9 %collective-permute-done = f32[4,128,128]{2,1,0:T(8,128)S(1)} collective-permute-done((f32[4,128,128]{2,1,0:T(8,128)}, f32[4,128,128]{2,1,0:T(8,128)S(1)}, u32[]{:S(2)}, u32[]{:S(2)}) %collective-permute-start) | collective-permute-done | bytes 262176 | tf_op jit(solution)/shard_map/while/body/eval_jaxpr/ppermute | solution.py:14
  161.5 10.1 %collective-permute-done = f32[4,128,128]{2,1,0:T(8,128)S(1)} collective-permute-done((f32[4,128,128]{2,1,0:T(8,128)}, f32[4,128,128]{2,1,0:T(8,128)S(1)}, u32[]{:S(2)}, u32[]{:S(2)}) %collective-permute-start) | collective-permute-done | bytes 262176 | tf_op jit(solution)/shard_map/while/body/eval_jaxpr/ppermute | solution.py:14
  175.2 9.9 %collective-permute-done = f32[4,128,128]{2,1,0:T(8,128)S(1)} collective-permute-done((f32[4,128,128]{2,1,0:T(8,128)}, f32[4,128,128]{2,1,0:T(8,128)S(1)}, u32[]{:S(2)}, u32[]{:S(2)}) %collective-permute-start) | collective-permute-done | bytes 262176 | tf_op jit(solution)/shard_map/while/body/eval_jaxpr/ppermute | solution.py:14
  188.6 9.9 %collective-permute-done = f32[4,128,128]{2,1,0:T(8,128)S(1)} collective-permute-done((f32[4,128,128]{2,1,0:T(8,128)}, f32[4,128,128]{2,1,0:T(8,128)S(1)}, u32[]{:S(2)}, u32[]{:S(2)}) %collective-permute-start) | collective-permute-done | bytes 262176 | tf_op jit(solution)/shard_map/while/body/eval_jaxpr/ppermute | solution.py:14
  229.0 9.9 %collective-permute-done = f32[4,128,128]{2,1,0:T(8,128)S(1)} collective-permute-done((f32[4,128,128]{2,1,0:T(8,128)}, f32[4,128,128]{2,1,0:T(8,128)S(1)}, u32[]{:S(2)}, u32[]{:S(2)}) %collective-permute-start) | collective-permute-done | bytes 262176 | tf_op jit(solution)/shard_map/while/body/eval_jaxpr/ppermute | solution.py:14
  242.5 9.9 %collective-permute-done = f32[4,128,128]{2,1,0:T(8,128)S(1)} collective-permute-done((f32[4,128,128]{2,1,0:T(8,128)}, f32[4,128,128]{2,1,0:T(8,128)S(1)}, u32[]{:S(2)}, u32[]{:S(2)}) %collective-permute-start) | collective-permute-done | bytes 262176 | tf_op jit(solution)/shard_map/while/body/eval_jaxpr/ppermute | solution.py:14
  256.0 10.7 %collective-permute-done = f32[4,128,128]{2,1,0:T(8,128)S(1)} collective-permute-done((f32[4,128,128]{2,1,0:T(8,128)}, f32[4,128,128]{2,1,0:T(8,128)S(1)}, u32[]{:S(2)}, u32[]{:S(2)}) %collective-permute-start) | collective-permute-done | bytes 262176 | tf_op jit(solution)/shard_map/while/body/eval_jaxpr/ppermute | solution.py:14
  270.3 11.8 %collective-permute-done = f32[4,128,128]{2,1,0:T(8,128)S(1)} collective-permute-done((f32[4,128,128]{2,1,0:T(8,128)}, f32[4,128,128]{2,1,0:T(8,128)S(1)}, u32[]{:S(2)}, u32[]{:S(2)}) %collective-permute-start) | collective-permute-done | bytes 262176 | tf_op jit(solution)/shard_map/while/body/eval_jaxpr/ppermute | solution.py:14
  285.7 12.4 %collective-permute-done = f32[4,128,128]{2,1,0:T(8,128)S(1)} collective-permute-done((f32[4,128,128]{2,1,0:T(8,128)}, f32[4,128,128]{2,1,0:T(8,128)S(1)}, u32[]{:S(2)}, u32[]{:S(2)}) %collective-permute-start) | collective-permute-done | bytes 262176 | tf_op jit(solution)/shard_map/while/body/eval_jaxpr/ppermute | solution.py:14
  301.7 11.5 %collective-permute-done = f32[4,128,128]{2,1,0:T(8,128)S(1)} collective-permute-done((f32[4,128,128]{2,1,0:T(8,128)}, f32[4,128,128]{2,1,0:T(8,128)S(1)}, u32[]{:S(2)}, u32[]{:S(2)}) %collective-permute-start) | collective-permute-done | bytes 262176 | tf_op jit(solution)/shard_map/while/body/eval_jaxpr/ppermute | solution.py:14
  316.8 10.6 %collective-permute-done = f32[4,128,128]{2,1,0:T(8,128)S(1)} collective-permute-done((f32[4,128,128]{2,1,0:T(8,128)}, f32[4,128,128]{2,1,0:T(8,128)S(1)}, u32[]{:S(2)}, u32[]{:S(2)}) %collective-permute-start) | collective-permute-done | bytes 262176 | tf_op jit(solution)/shard_map/while/body/eval_jaxpr/ppermute | solution.py:14
  344.5 9.9 %collective-permute-done = f32[4,128,128]{2,1,0:T(8,128)S(1)} collective-permute-done((f32[4,128,128]{2,1,0:T(8,128)}, f32[4,128,128]{2,1,0:T(8,128)S(1)}, u32[]{:S(2)}, u32[]{:S(2)}) %collective-permute-start) | collective-permute-done | bytes 262176 | tf_op jit(solution)/shard_map/while/body/eval_jaxpr/ppermute | solution.py:14
  357.9 9.9 %collective-permute-done = f32[4,128,128]{2,1,0:T(8,128)S(1)} collective-permute-done((f32[4,128,128]{2,1,0:T(8,128)}, f32[4,128,128]{2,1,0:T(8,128)S(1)}, u32[]{:S(2)}, u32[]{:S(2)}) %collective-permute-start) | collective-permute-done | bytes 262176 | tf_op jit(solution)/shard_map/while/body/eval_jaxpr/ppermute | solution.py:14
  371.4 9.9 %collective-permute-done = f32[4,128,128]{2,1,0:T(8,128)S(1)} collective-permute-done((f32[4,128,128]{2,1,0:T(8,128)}, f32[4,128,128]{2,1,0:T(8,128)S(1)}, u32[]{:S(2)}, u32[]{:S(2)}) %collective-permute-start) | collective-permute-done | bytes 262176 | tf_op jit(solution)/shard_map/while/body/eval_jaxpr/ppermute | solution.py:14
  411.8 10.1 %collective-permute-done = f32[4,128,128]{2,1,0:T(8,128)S(1)} collective-permute-done((f32[4,128,128]{2,1,0:T(8,128)}, f32[4,128,128]{2,1,0:T(8,128)S(1)}, u32[]{:S(2)}, u32[]{:S(2)}) %collective-permute-start) | collective-permute-done | bytes 262176 | tf_op jit(solution)/shard_map/while/body/eval_jaxpr/ppermute | solution.py:14
  425.6 11.3 %collective-permute-done = f32[4,128,128]{2,1,0:T(8,128)S(1)} collective-permute-done((f32[4,128,128]{2,1,0:T(8,128)}, f32[4,128,128]{2,1,0:T(8,128)S(1)}, u32[]{:S(2)}, u32[]{:S(2)}) %collective-permute-start) | collective-permute-done | bytes 262176 | tf_op jit(solution)/shard_map/while/body/eval_jaxpr/ppermute | solution.py:14
  440.4 9.9 %collective-permute-done = f32[4,128,128]{2,1,0:T(8,128)S(1)} collective-permute-done((f32[4,128,128]{2,1,0:T(8,128)}, f32[4,128,128]{2,1,0:T(8,128)S(1)}, u32[]{:S(2)}, u32[]{:S(2)}) %collective-permute-start) | collective-permute-done | bytes 262176 | tf_op jit(solution)/shard_map/while/body/eval_jaxpr/ppermute | solution.py:14
  (117 shorter events, 243.2 us)
Async XLA Ops:
  43.8 11.8 %collective-permute-start = (f32[4,128,128]{2,1,0:T(8,128)}, f32[4,128,128]{2,1,0:T(8,128)S(1)}, u32[]{:S(2)}, u32[]{:S(2)}) collective-permute-start(f32[4,128,128]{2,1,0:T(8,128)} %add.116), channel_id=1, source_target_pairs={{0,8},{8,16},{16,24},{24,32},{32,40},{40,48},{48,56},{56,64},{64,7... | collective-permute-start | bytes 786440 | tf_op jit(solution)/shard_map/while/body/eval_jaxpr/ppermute | solution.py:14
  57.3 11.8 %collective-permute-start = (f32[4,128,128]{2,1,0:T(8,128)}, f32[4,128,128]{2,1,0:T(8,128)S(1)}, u32[]{:S(2)}, u32[]{:S(2)}) collective-permute-start(f32[4,128,128]{2,1,0:T(8,128)} %add.116), channel_id=1, source_target_pairs={{0,8},{8,16},{16,24},{24,32},{32,40},{40,48},{48,56},{56,64},{64,7... | collective-permute-start | bytes 786440 | tf_op jit(solution)/shard_map/while/body/eval_jaxpr/ppermute | solution.py:14
  70.8 11.8 %collective-permute-start = (f32[4,128,128]{2,1,0:T(8,128)}, f32[4,128,128]{2,1,0:T(8,128)S(1)}, u32[]{:S(2)}, u32[]{:S(2)}) collective-permute-start(f32[4,128,128]{2,1,0:T(8,128)} %add.116), channel_id=1, source_target_pairs={{0,8},{8,16},{16,24},{24,32},{32,40},{40,48},{48,56},{56,64},{64,7... | collective-permute-start | bytes 786440 | tf_op jit(solution)/shard_map/while/body/eval_jaxpr/ppermute | solution.py:14
  84.2 12.3 %collective-permute-start = (f32[4,128,128]{2,1,0:T(8,128)}, f32[4,128,128]{2,1,0:T(8,128)S(1)}, u32[]{:S(2)}, u32[]{:S(2)}) collective-permute-start(f32[4,128,128]{2,1,0:T(8,128)} %add.116), channel_id=1, source_target_pairs={{0,8},{8,16},{16,24},{24,32},{32,40},{40,48},{48,56},{56,64},{64,7... | collective-permute-start | bytes 786440 | tf_op jit(solution)/shard_map/while/body/eval_jaxpr/ppermute | solution.py:14
  98.2 13.5 %collective-permute-start = (f32[4,128,128]{2,1,0:T(8,128)}, f32[4,128,128]{2,1,0:T(8,128)S(1)}, u32[]{:S(2)}, u32[]{:S(2)}) collective-permute-start(f32[4,128,128]{2,1,0:T(8,128)} %add.116), channel_id=1, source_target_pairs={{0,8},{8,16},{16,24},{24,32},{32,40},{40,48},{48,56},{56,64},{64,7... | collective-permute-start | bytes 786440 | tf_op jit(solution)/shard_map/while/body/eval_jaxpr/ppermute | solution.py:14
  113.4 14.6 %collective-permute-start = (f32[4,128,128]{2,1,0:T(8,128)}, f32[4,128,128]{2,1,0:T(8,128)S(1)}, u32[]{:S(2)}, u32[]{:S(2)}) collective-permute-start(f32[4,128,128]{2,1,0:T(8,128)} %add.116), channel_id=1, source_target_pairs={{0,8},{8,16},{16,24},{24,32},{32,40},{40,48},{48,56},{56,64},{64,7... | collective-permute-start | bytes 786440 | tf_op jit(solution)/shard_map/while/body/eval_jaxpr/ppermute | solution.py:14
  129.6 13.7 %collective-permute-start = (f32[4,128,128]{2,1,0:T(8,128)}, f32[4,128,128]{2,1,0:T(8,128)S(1)}, u32[]{:S(2)}, u32[]{:S(2)}) collective-permute-start(f32[4,128,128]{2,1,0:T(8,128)} %add.116), channel_id=1, source_target_pairs={{0,8},{8,16},{16,24},{24,32},{32,40},{40,48},{48,56},{56,64},{64,7... | collective-permute-start | bytes 786440 | tf_op jit(solution)/shard_map/while/body/eval_jaxpr/ppermute | solution.py:14
  145.0 12.9 %collective-permute-start = (f32[4,128,128]{2,1,0:T(8,128)}, f32[4,128,128]{2,1,0:T(8,128)S(1)}, u32[]{:S(2)}, u32[]{:S(2)}) collective-permute-start(f32[4,128,128]{2,1,0:T(8,128)} %add.116), channel_id=1, source_target_pairs={{0,8},{8,16},{16,24},{24,32},{32,40},{40,48},{48,56},{56,64},{64,7... | collective-permute-start | bytes 786440 | tf_op jit(solution)/shard_map/while/body/eval_jaxpr/ppermute | solution.py:14
  159.6 12.0 %collective-permute-start = (f32[4,128,128]{2,1,0:T(8,128)}, f32[4,128,128]{2,1,0:T(8,128)S(1)}, u32[]{:S(2)}, u32[]{:S(2)}) collective-permute-start(f32[4,128,128]{2,1,0:T(8,128)} %add.116), channel_id=1, source_target_pairs={{0,8},{8,16},{16,24},{24,32},{32,40},{40,48},{48,56},{56,64},{64,7... | collective-permute-start | bytes 786440 | tf_op jit(solution)/shard_map/while/body/eval_jaxpr/ppermute | solution.py:14
  173.3 11.8 %collective-permute-start = (f32[4,128,128]{2,1,0:T(8,128)}, f32[4,128,128]{2,1,0:T(8,128)S(1)}, u32[]{:S(2)}, u32[]{:S(2)}) collective-permute-start(f32[4,128,128]{2,1,0:T(8,128)} %add.116), channel_id=1, source_target_pairs={{0,8},{8,16},{16,24},{24,32},{32,40},{40,48},{48,56},{56,64},{64,7... | collective-permute-start | bytes 786440 | tf_op jit(solution)/shard_map/while/body/eval_jaxpr/ppermute | solution.py:14
  186.7 11.8 %collective-permute-start = (f32[4,128,128]{2,1,0:T(8,128)}, f32[4,128,128]{2,1,0:T(8,128)S(1)}, u32[]{:S(2)}, u32[]{:S(2)}) collective-permute-start(f32[4,128,128]{2,1,0:T(8,128)} %add.116), channel_id=1, source_target_pairs={{0,8},{8,16},{16,24},{24,32},{32,40},{40,48},{48,56},{56,64},{64,7... | collective-permute-start | bytes 786440 | tf_op jit(solution)/shard_map/while/body/eval_jaxpr/ppermute | solution.py:14
  200.2 11.8 %collective-permute-start = (f32[4,128,128]{2,1,0:T(8,128)}, f32[4,128,128]{2,1,0:T(8,128)S(1)}, u32[]{:S(2)}, u32[]{:S(2)}) collective-permute-start(f32[4,128,128]{2,1,0:T(8,128)} %add.116), channel_id=1, source_target_pairs={{0,8},{8,16},{16,24},{24,32},{32,40},{40,48},{48,56},{56,64},{64,7... | collective-permute-start | bytes 786440 | tf_op jit(solution)/shard_map/while/body/eval_jaxpr/ppermute | solution.py:14
  213.7 11.8 %collective-permute-start = (f32[4,128,128]{2,1,0:T(8,128)}, f32[4,128,128]{2,1,0:T(8,128)S(1)}, u32[]{:S(2)}, u32[]{:S(2)}) collective-permute-start(f32[4,128,128]{2,1,0:T(8,128)} %add.116), channel_id=1, source_target_pairs={{0,8},{8,16},{16,24},{24,32},{32,40},{40,48},{48,56},{56,64},{64,7... | collective-permute-start | bytes 786440 | tf_op jit(solution)/shard_map/while/body/eval_jaxpr/ppermute | solution.py:14
  227.1 11.8 %collective-permute-start = (f32[4,128,128]{2,1,0:T(8,128)}, f32[4,128,128]{2,1,0:T(8,128)S(1)}, u32[]{:S(2)}, u32[]{:S(2)}) collective-permute-start(f32[4,128,128]{2,1,0:T(8,128)} %add.116), channel_id=1, source_target_pairs={{0,8},{8,16},{16,24},{24,32},{32,40},{40,48},{48,56},{56,64},{64,7... | collective-permute-start | bytes 786440 | tf_op jit(solution)/shard_map/while/body/eval_jaxpr/ppermute | solution.py:14
  240.6 11.8 %collective-permute-start = (f32[4,128,128]{2,1,0:T(8,128)}, f32[4,128,128]{2,1,0:T(8,128)S(1)}, u32[]{:S(2)}, u32[]{:S(2)}) collective-permute-start(f32[4,128,128]{2,1,0:T(8,128)} %add.116), channel_id=1, source_target_pairs={{0,8},{8,16},{16,24},{24,32},{32,40},{40,48},{48,56},{56,64},{64,7... | collective-permute-start | bytes 786440 | tf_op jit(solution)/shard_map/while/body/eval_jaxpr/ppermute | solution.py:14
  254.1 12.6 %collective-permute-start = (f32[4,128,128]{2,1,0:T(8,128)}, f32[4,128,128]{2,1,0:T(8,128)S(1)}, u32[]{:S(2)}, u32[]{:S(2)}) collective-permute-start(f32[4,128,128]{2,1,0:T(8,128)} %add.116), channel_id=1, source_target_pairs={{0,8},{8,16},{16,24},{24,32},{32,40},{40,48},{48,56},{56,64},{64,7... | collective-permute-start | bytes 786440 | tf_op jit(solution)/shard_map/while/body/eval_jaxpr/ppermute | solution.py:14
  268.4 13.8 %collective-permute-start = (f32[4,128,128]{2,1,0:T(8,128)}, f32[4,128,128]{2,1,0:T(8,128)S(1)}, u32[]{:S(2)}, u32[]{:S(2)}) collective-permute-start(f32[4,128,128]{2,1,0:T(8,128)} %add.116), channel_id=1, source_target_pairs={{0,8},{8,16},{16,24},{24,32},{32,40},{40,48},{48,56},{56,64},{64,7... | collective-permute-start | bytes 786440 | tf_op jit(solution)/shard_map/while/body/eval_jaxpr/ppermute | solution.py:14
  283.8 14.3 %collective-permute-start = (f32[4,128,128]{2,1,0:T(8,128)}, f32[4,128,128]{2,1,0:T(8,128)S(1)}, u32[]{:S(2)}, u32[]{:S(2)}) collective-permute-start(f32[4,128,128]{2,1,0:T(8,128)} %add.116), channel_id=1, source_target_pairs={{0,8},{8,16},{16,24},{24,32},{32,40},{40,48},{48,56},{56,64},{64,7... | collective-permute-start | bytes 786440 | tf_op jit(solution)/shard_map/while/body/eval_jaxpr/ppermute | solution.py:14
  299.8 13.4 %collective-permute-start = (f32[4,128,128]{2,1,0:T(8,128)}, f32[4,128,128]{2,1,0:T(8,128)S(1)}, u32[]{:S(2)}, u32[]{:S(2)}) collective-permute-start(f32[4,128,128]{2,1,0:T(8,128)} %add.116), channel_id=1, source_target_pairs={{0,8},{8,16},{16,24},{24,32},{32,40},{40,48},{48,56},{56,64},{64,7... | collective-permute-start | bytes 786440 | tf_op jit(solution)/shard_map/while/body/eval_jaxpr/ppermute | solution.py:14
  314.9 12.6 %collective-permute-start = (f32[4,128,128]{2,1,0:T(8,128)}, f32[4,128,128]{2,1,0:T(8,128)S(1)}, u32[]{:S(2)}, u32[]{:S(2)}) collective-permute-start(f32[4,128,128]{2,1,0:T(8,128)} %add.116), channel_id=1, source_target_pairs={{0,8},{8,16},{16,24},{24,32},{32,40},{40,48},{48,56},{56,64},{64,7... | collective-permute-start | bytes 786440 | tf_op jit(solution)/shard_map/while/body/eval_jaxpr/ppermute | solution.py:14
  369.5 11.8 %collective-permute-start = (f32[4,128,128]{2,1,0:T(8,128)}, f32[4,128,128]{2,1,0:T(8,128)S(1)}, u32[]{:S(2)}, u32[]{:S(2)}) collective-permute-start(f32[4,128,128]{2,1,0:T(8,128)} %add.116), channel_id=1, source_target_pairs={{0,8},{8,16},{16,24},{24,32},{32,40},{40,48},{48,56},{56,64},{64,7... | collective-permute-start | bytes 786440 | tf_op jit(solution)/shard_map/while/body/eval_jaxpr/ppermute | solution.py:14
  409.9 12.1 %collective-permute-start = (f32[4,128,128]{2,1,0:T(8,128)}, f32[4,128,128]{2,1,0:T(8,128)S(1)}, u32[]{:S(2)}, u32[]{:S(2)}) collective-permute-start(f32[4,128,128]{2,1,0:T(8,128)} %add.116), channel_id=1, source_target_pairs={{0,8},{8,16},{16,24},{24,32},{32,40},{40,48},{48,56},{56,64},{64,7... | collective-permute-start | bytes 786440 | tf_op jit(solution)/shard_map/while/body/eval_jaxpr/ppermute | solution.py:14
  423.6 13.2 %collective-permute-start = (f32[4,128,128]{2,1,0:T(8,128)}, f32[4,128,128]{2,1,0:T(8,128)S(1)}, u32[]{:S(2)}, u32[]{:S(2)}) collective-permute-start(f32[4,128,128]{2,1,0:T(8,128)} %add.116), channel_id=1, source_target_pairs={{0,8},{8,16},{16,24},{24,32},{32,40},{40,48},{48,56},{56,64},{64,7... | collective-permute-start | bytes 786440 | tf_op jit(solution)/shard_map/while/body/eval_jaxpr/ppermute | solution.py:14
  438.5 11.8 %collective-permute-start = (f32[4,128,128]{2,1,0:T(8,128)}, f32[4,128,128]{2,1,0:T(8,128)S(1)}, u32[]{:S(2)}, u32[]{:S(2)}) collective-permute-start(f32[4,128,128]{2,1,0:T(8,128)} %add.116), channel_id=1, source_target_pairs={{0,8},{8,16},{16,24},{24,32},{32,40},{40,48},{48,56},{56,64},{64,7... | collective-permute-start | bytes 786440 | tf_op jit(solution)/shard_map/while/body/eval_jaxpr/ppermute | solution.py:14
  (20 other events, 189.9 us)
